TPU v7x, 512 devices: a whole 4x4x16 slice. The times are simulated.
512 devices in a mesh: band: 32 (over x, z_lo), grid: 16 (over z_hi, y, core).
Axes of the slice: x: 4, y: 4, z: 16 (z_hi: 2, z_lo: 8; z = z_hi * 8 + z_lo), core: 2. Of those that a mesh axis runs over, the one named last changes fastest.
Arguments:
- trial_bands: float32 [64, 160, 32, 128], P('band', 'grid'), may hold values from -6 to 6
- potential: float32 [160, 32, 128], P('grid'), may hold values from -2 to 0
Outputs:
- filtered: float32 [64, 160, 32, 128], P('band', 'grid')
- projected: float32 [64, 64], P('band')
- residual_norms: float32 [64], P('band')
All inputs are finite; a program needn't handle non-finite values.
Results may differ from a plain program's by a relative error of at most 0.00016.
Values sent between devices are 32-bit elements; how exact they have to be, the bound alone decides.
No kernel may reach another device: no remote copies, remote signals or barrier semaphores. Data moves between devices by JAX's collectives and lax.ppermute only.
A program may use at most 64 MiB of HBM per device.

v0:
```python
import jax
import jax.numpy as jnp
from jax import lax
from jax.sharding import PartitionSpec as P

CENTER = 4.25
HALF_WIDTH = 3.75
LOWEST = -2.0
SIGMA_ONE = HALF_WIDTH / (LOWEST - CENTER)
FOUR_THIRDS = 4.0 / 3.0
TWELFTH = 1.0 / 12.0
filter_degree = 4


def padded_2(cells, sides, width):
    for axis, dim in sides:
        count = lax.axis_size(axis)
        head = lax.slice_in_dim(cells, 0, width, axis=dim)
        tail = lax.slice_in_dim(cells, cells.shape[dim] - width, cells.shape[dim], axis=dim)
        cells = jnp.concatenate(
            [
                lax.ppermute(tail, axis, [(i, (i + 1) % count) for i in range(count)]),
                cells,
                lax.ppermute(head, axis, [((i + 1) % count, i) for i in range(count)]),
            ],
            axis=dim,
        )
    return cells


def operate(field_in, potential):
    padded = padded_2(field_in, (("grid", 1),), 2)
    plane_count = field_in.shape[1]
    near_sum = padded[:, 1 : 1 + plane_count] + padded[:, 3 : 3 + plane_count]
    near_sum = near_sum + jnp.roll(field_in, 1, 2) + jnp.roll(field_in, -1, 2)
    near_sum = near_sum + jnp.roll(field_in, 1, 3) + jnp.roll(field_in, -1, 3)
    far_sum = padded[:, 0:plane_count] + padded[:, 4 : 4 + plane_count]
    far_sum = far_sum + jnp.roll(field_in, 2, 2) + jnp.roll(field_in, -2, 2)
    far_sum = far_sum + jnp.roll(field_in, 2, 3) + jnp.roll(field_in, -2, 3)
    kinetic = 0.5 * (7.5 * field_in - FOUR_THIRDS * near_sum + TWELFTH * far_sum)
    return kinetic + potential * field_in


def on_device(trial_bands, potential):
    sigma_now = SIGMA_ONE
    previous = trial_bands
    current = (operate(trial_bands, potential) - CENTER * trial_bands) * (SIGMA_ONE / HALF_WIDTH)
    for repeat_index in range(filter_degree - 1):
        sigma_next = 1.0 / (2.0 / SIGMA_ONE - sigma_now)
        following = (operate(current, potential) - CENTER * current) * (
            2.0 * sigma_next / HALF_WIDTH
        ) - sigma_now * sigma_next * previous
        previous, current, sigma_now = (current, following, sigma_next)
    applied = operate(current, potential)
    band_count = current.shape[0]
    band_devices = lax.axis_size("band")
    total_bands = band_count * band_devices
    cell_count = current.shape[1] * current.shape[2] * current.shape[3]
    cell_total = cell_count * lax.axis_size("grid")
    inverse_cells = 1.0 / cell_total
    first_band = lax.axis_index("band") * band_count
    both = jnp.stack(
        [current.reshape(band_count, cell_count), applied.reshape(band_count, cell_count)]
    ).reshape(2, band_count, band_devices, cell_count // band_devices)
    moved = lax.all_to_all(both, "band", 2, 1, tiled=True)
    bands_here = moved[0].reshape(total_bands, -1)
    image_here = moved[1].reshape(total_bands, -1)
    margin_part = jnp.dot(
        bands_here,
        bands_here.T,
        precision=lax.Precision.HIGHEST,
        preferred_element_type=jnp.float32,
    )
    image_part = jnp.dot(
        image_here,
        bands_here.T,
        precision=lax.Precision.HIGHEST,
        preferred_element_type=jnp.float32,
    )
    norm_part = jnp.sum(image_here * image_here, axis=1)
    packed = jnp.concatenate([margin_part.reshape(-1), image_part.reshape(-1), norm_part])
    packed = lax.psum(packed, ("band", "grid")) * inverse_cells
    square = total_bands * total_bands
    margin = packed[:square].reshape(total_bands, total_bands)
    subspace = packed[square : 2 * square].reshape(total_bands, total_bands)
    image_norms = packed[2 * square :]
    factor = jnp.linalg.cholesky(margin)
    coefficients = lax.linalg.triangular_solve(factor, subspace.T, left_side=True, lower=True)
    projected = lax.linalg.triangular_solve(factor, coefficients.T, left_side=True, lower=True)
    residual_norms = image_norms - jnp.sum(coefficients * coefficients, axis=0)
    projected_rows = lax.dynamic_slice_in_dim(projected, first_band, band_count, 0)
    residual_rows = lax.dynamic_slice_in_dim(residual_norms, first_band, band_count, 0)
    return (current, projected_rows, residual_rows)


def solution(mesh):
    in_specs = (P("band", "grid", None, None), P("grid", None, None))
    out_specs = (P("band", "grid", None, None), P("band", None), P("band"))
    return jax.shard_map(
        on_device, mesh=mesh, in_specs=in_specs, out_specs=out_specs, check_vma=False
    )
```

profile of v0, /device:TPU:1, one launch (start us, length us, event | category | flops | bytes accessed | tf_op | source)
XLA Modules:
  0.0 275.6 jit_solution(5035472801133282586)
XLA Ops:
  0.6 0.9 fusion.146
  1.5 4.6 %collective-permute-start = (f32[2,2,32,128]{3,2,1,0:T(8,128)S(1)}, f32[2,2,32,128]{3,2,1,0:T(8,128)S(1)}, u32[]{:S(2)}, u32[]{:S(2)}) collective-permute-start(f32[2,2,32,128]{3,2,1,0:T(8,128)S(1)} %get-tuple-element.91), channel_id=1, source_target_pairs={{0,1},{1,2},{2,3},{3,4},{4,5},{5,6},{6,7},{7,8},{8,9},{9,10},{10,1... | collective-permute-start | bytes 196616 | tf_op jit(solution)/shard_map/ppermute | solution.py:22
  6.1 6.2 %collective-permute-start.1 = (f32[2,2,32,128]{3,2,1,0:T(8,128)S(1)}, f32[2,2,32,128]{3,2,1,0:T(8,128)S(1)}, u32[]{:S(2)}, u32[]{:S(2)}) collective-permute-start(f32[2,2,32,128]{3,2,1,0:T(8,128)S(1)} %get-tuple-element.92), channel_id=1, source_target_pairs={{1,0},{2,1},{3,2},{4,3},{5,4},{6,5},{7,6},{8,7},{9,8},{10,9},{11,1... | collective-permute-start | bytes 196616 | tf_op jit(solution)/shard_map/ppermute | solution.py:24
  12.4 1.2 fusion.150
  13.8 0.2 fusion.145
  14.3 0.7 copy-done.2
  15.2 0.7 broadcast_multiply_fusion
  16.0 0.2 fusion.134
  16.4 0.2 fusion.138
  16.7 1.9 collective-permute-start.2
  18.6 14.5 %collective-permute-start.3 = (f32[2,2,32,128]{3,2,1,0:T(8,128)S(1)}, f32[2,2,32,128]{3,2,1,0:T(8,128)S(1)}, u32[]{:S(2)}, u32[]{:S(2)}) collective-permute-start(f32[2,2,32,128]{3,2,1,0:T(8,128)S(1)} %get-tuple-element.80), channel_id=1, source_target_pairs={{1,0},{2,1},{3,2},{4,3},{5,4},{6,5},{7,6},{8,7},{9,8},{10,9},{11,1... | collective-permute-start | bytes 196616 | tf_op jit(solution)/shard_map/ppermute | solution.py:24
  33.1 0.8 collective-permute-done.3
  34.0 0.7 fusion.55
  35.5 1.9 collective-permute-start.4
  37.4 15.5 %collective-permute-start.5 = (f32[2,2,32,128]{3,2,1,0:T(8,128)S(1)}, f32[2,2,32,128]{3,2,1,0:T(8,128)S(1)}, u32[]{:S(2)}, u32[]{:S(2)}) collective-permute-start(f32[2,2,32,128]{3,2,1,0:T(8,128)S(1)} %get-tuple-element.62), channel_id=1, source_target_pairs={{1,0},{2,1},{3,2},{4,3},{5,4},{6,5},{7,6},{8,7},{9,8},{10,9},{11,1... | collective-permute-start | bytes 196616 | tf_op jit(solution)/shard_map/ppermute | solution.py:24
  52.9 0.8 collective-permute-done.5
  53.8 0.6 fusion.40
  55.2 1.9 collective-permute-start.6
  57.2 15.5 %collective-permute-start.7 = (f32[2,2,32,128]{3,2,1,0:T(8,128)S(1)}, f32[2,2,32,128]{3,2,1,0:T(8,128)S(1)}, u32[]{:S(2)}, u32[]{:S(2)}) collective-permute-start(f32[2,2,32,128]{3,2,1,0:T(8,128)S(1)} %get-tuple-element.44), channel_id=1, source_target_pairs={{1,0},{2,1},{3,2},{4,3},{5,4},{6,5},{7,6},{8,7},{9,8},{10,9},{11,1... | collective-permute-start | bytes 196616 | tf_op jit(solution)/shard_map/ppermute | solution.py:24
  72.7 0.8 collective-permute-done.7
  73.6 0.6 fusion.25
  74.8 0.9 fusion.111
  75.7 0.9 fusion.112
  76.6 0.7 fusion.114
  77.3 1.9 collective-permute-start.8
  79.2 15.5 %collective-permute-start.9 = (f32[2,2,32,128]{3,2,1,0:T(8,128)}, f32[2,2,32,128]{3,2,1,0:T(8,128)}, u32[]{:S(2)}, u32[]{:S(2)}) collective-permute-start(f32[2,2,32,128]{3,2,1,0:T(8,128)} %get-tuple-element.26), channel_id=1, source_target_pairs={{1,0},{2,1},{3,2},{4,3},{5,4},{6,5},{7,6},{8,7},{9,8},{10,9},{11,1... | collective-permute-start | bytes 196616 | tf_op jit(solution)/shard_map/ppermute | solution.py:24
  94.7 0.6 fusion.113
  95.4 0.8 stack.7
  96.2 0.7 copy-done.4
  96.9 2.5 fusion.10
  99.4 1.1 stack.8
  100.5 1.4 copy.10
  101.9 10.4 %all-to-all-start = ((f32[2,2,32,1280]{3,1,0,2:T(2,128)}), f32[2,2,32,1280]{3,1,0,2:T(2,128)S(1)}, u32[]{:S(2)}, u32[]{:S(2)}) async-start(f32[2,2,32,1280]{3,1,0,2:T(2,128)} %copy.10), calls=%async_computation | async-start | bytes 1310720 | tf_op jit(solution)/shard_map/all_to_all | solution.py:65
  112.3 22.4 %all-to-all-done = f32[2,2,32,1280]{3,1,0,2:T(2,128)S(1)} async-done(((f32[2,2,32,1280]{3,1,0,2:T(2,128)}), f32[2,2,32,1280]{3,1,0,2:T(2,128)S(1)}, u32[]{:S(2)}, u32[]{:S(2)}) %all-to-all-start) | async-done | bytes 655392 | tf_op jit(solution)/shard_map/all_to_all | solution.py:65
  134.7 0.3 fusion.105
  135.0 0.2 reshape_squeeze.6
  135.2 0.2 reshape_squeeze.7
  135.4 0.4 fusion.152
  135.8 0.4 fusion.153
  136.5 125.1 %psum.7 = f32[8256]{0:T(1024)S(1)} all-reduce(f32[8256]{0:T(1024)S(1)} %pad_maximum_fusion.9), channel_id=1, replica_groups=mesh['band'=32,'grid'=16] {'band','grid'}, use_global_device_ids=true, to_apply=%region_1.2 | all-reduce | flops 8256 | bytes 66048 | tf_op jit(solution)/shard_map/psum | solution.py:82
  261.8 5.8 %cholesky.18 = f32[64,64]{1,0:T(8,128)S(1)} custom-call(f32[64,64]{1,0:T(8,128)S(1)} %fusion.103), custom_call_target="Cholesky" | custom-call | tf_op jit(solution)/shard_map/jit(cholesky)/cholesky | solution.py:87
  267.7 0.6 compare_reduce_fusion
  268.3 0.7 fusion.96
  269.0 4.9 %custom-call.8 = f32[1,64,64]{1,2,0:T(8,128)S(1)} custom-call(f32[1,64,64]{2,1,0:T(8,128)S(1)} %fusion.96), custom_call_target="InvertDiagBlocksLowerTriangular" | custom-call | tf_op jit(solution)/shard_map/triangular_solve/custom-call.0 | solution.py:89
  273.9 0.3 multiply_reduce_fusion.1
  274.2 0.2 fusion.97
  274.4 0.6 dynamic_slice.7
  275.0 0.6 constant_dynamic-slice_fusion
  (70 shorter events, 3.9 us)
Async XLA Ops:
  1.5 13.5 %collective-permute-start = (f32[2,2,32,128]{3,2,1,0:T(8,128)S(1)}, f32[2,2,32,128]{3,2,1,0:T(8,128)S(1)}, u32[]{:S(2)}, u32[]{:S(2)}) collective-permute-start(f32[2,2,32,128]{3,2,1,0:T(8,128)S(1)} %get-tuple-element.91), channel_id=1, source_target_pairs={{0,1},{1,2},{2,3},{3,4},{4,5},{5,6},{6,7},{7,8},{8,9},{9,10},{10,1... | collective-permute-start | bytes 196616 | tf_op jit(solution)/shard_map/ppermute | solution.py:22
  6.1 7.5 %copy-start.1 = (f32[2,10,32,128]{3,2,1,0:T(8,128)S(1)}, f32[2,10,32,128]{3,2,1,0:T(8,128)}, u32[]{:S(2)}) copy-start(f32[2,10,32,128]{3,2,1,0:T(8,128)} %param.4) | copy-start | bytes 983044
  6.1 9.0 %collective-permute-start.1 = (f32[2,2,32,128]{3,2,1,0:T(8,128)S(1)}, f32[2,2,32,128]{3,2,1,0:T(8,128)S(1)}, u32[]{:S(2)}, u32[]{:S(2)}) collective-permute-start(f32[2,2,32,128]{3,2,1,0:T(8,128)S(1)} %get-tuple-element.92), channel_id=1, source_target_pairs={{1,0},{2,1},{3,2},{4,3},{5,4},{6,5},{7,6},{8,7},{9,8},{10,9},{11,1... | collective-permute-start | bytes 196616 | tf_op jit(solution)/shard_map/ppermute | solution.py:24
  14.1 0.9 copy-start.2
  16.7 16.4 %collective-permute-start.2 = (f32[2,2,32,128]{3,2,1,0:T(8,128)S(1)}, f32[2,2,32,128]{3,2,1,0:T(8,128)S(1)}, u32[]{:S(2)}, u32[]{:S(2)}) collective-permute-start(f32[2,2,32,128]{3,2,1,0:T(8,128)S(1)} %get-tuple-element.79), channel_id=1, source_target_pairs={{0,1},{1,2},{2,3},{3,4},{4,5},{5,6},{6,7},{7,8},{8,9},{9,10},{10,1... | collective-permute-start | bytes 196616 | tf_op jit(solution)/shard_map/ppermute | solution.py:22
  18.6 15.4 %collective-permute-start.3 = (f32[2,2,32,128]{3,2,1,0:T(8,128)S(1)}, f32[2,2,32,128]{3,2,1,0:T(8,128)S(1)}, u32[]{:S(2)}, u32[]{:S(2)}) collective-permute-start(f32[2,2,32,128]{3,2,1,0:T(8,128)S(1)} %get-tuple-element.80), channel_id=1, source_target_pairs={{1,0},{2,1},{3,2},{4,3},{5,4},{6,5},{7,6},{8,7},{9,8},{10,9},{11,1... | collective-permute-start | bytes 196616 | tf_op jit(solution)/shard_map/ppermute | solution.py:24
  35.5 17.4 %collective-permute-start.4 = (f32[2,2,32,128]{3,2,1,0:T(8,128)S(1)}, f32[2,2,32,128]{3,2,1,0:T(8,128)S(1)}, u32[]{:S(2)}, u32[]{:S(2)}) collective-permute-start(f32[2,2,32,128]{3,2,1,0:T(8,128)S(1)} %get-tuple-element.61), channel_id=1, source_target_pairs={{0,1},{1,2},{2,3},{3,4},{4,5},{5,6},{6,7},{7,8},{8,9},{9,10},{10,1... | collective-permute-start | bytes 196616 | tf_op jit(solution)/shard_map/ppermute | solution.py:22
  37.4 16.4 %collective-permute-start.5 = (f32[2,2,32,128]{3,2,1,0:T(8,128)S(1)}, f32[2,2,32,128]{3,2,1,0:T(8,128)S(1)}, u32[]{:S(2)}, u32[]{:S(2)}) collective-permute-start(f32[2,2,32,128]{3,2,1,0:T(8,128)S(1)} %get-tuple-element.62), channel_id=1, source_target_pairs={{1,0},{2,1},{3,2},{4,3},{5,4},{6,5},{7,6},{8,7},{9,8},{10,9},{11,1... | collective-permute-start | bytes 196616 | tf_op jit(solution)/shard_map/ppermute | solution.py:24
  55.2 17.5 %collective-permute-start.6 = (f32[2,2,32,128]{3,2,1,0:T(8,128)S(1)}, f32[2,2,32,128]{3,2,1,0:T(8,128)S(1)}, u32[]{:S(2)}, u32[]{:S(2)}) collective-permute-start(f32[2,2,32,128]{3,2,1,0:T(8,128)S(1)} %get-tuple-element.43), channel_id=1, source_target_pairs={{0,1},{1,2},{2,3},{3,4},{4,5},{5,6},{6,7},{7,8},{8,9},{9,10},{10,1... | collective-permute-start | bytes 196616 | tf_op jit(solution)/shard_map/ppermute | solution.py:22
  57.2 16.4 %collective-permute-start.7 = (f32[2,2,32,128]{3,2,1,0:T(8,128)S(1)}, f32[2,2,32,128]{3,2,1,0:T(8,128)S(1)}, u32[]{:S(2)}, u32[]{:S(2)}) collective-permute-start(f32[2,2,32,128]{3,2,1,0:T(8,128)S(1)} %get-tuple-element.44), channel_id=1, source_target_pairs={{1,0},{2,1},{3,2},{4,3},{5,4},{6,5},{7,6},{8,7},{9,8},{10,9},{11,1... | collective-permute-start | bytes 196616 | tf_op jit(solution)/shard_map/ppermute | solution.py:24
  74.2 21.9 %copy-start = (f32[2,10,32,128]{3,2,1,0:T(8,128)}, f32[2,10,32,128]{3,2,1,0:T(8,128)S(1)}, u32[]{:S(2)}) copy-start(f32[2,10,32,128]{3,2,1,0:T(8,128)S(1)} %fusion.25) | copy-start | bytes 983044
  77.3 18.9 %collective-permute-start.8 = (f32[2,2,32,128]{3,2,1,0:T(8,128)}, f32[2,2,32,128]{3,2,1,0:T(8,128)S(1)}, u32[]{:S(2)}, u32[]{:S(2)}) collective-permute-start(f32[2,2,32,128]{3,2,1,0:T(8,128)} %get-tuple-element.25), channel_id=1, source_target_pairs={{0,1},{1,2},{2,3},{3,4},{4,5},{5,6},{6,7},{7,8},{8,9},{9,10},{10,1... | collective-permute-start | bytes 196616 | tf_op jit(solution)/shard_map/ppermute | solution.py:22
  79.2 16.9 %collective-permute-start.9 = (f32[2,2,32,128]{3,2,1,0:T(8,128)}, f32[2,2,32,128]{3,2,1,0:T(8,128)}, u32[]{:S(2)}, u32[]{:S(2)}) collective-permute-start(f32[2,2,32,128]{3,2,1,0:T(8,128)} %get-tuple-element.26), channel_id=1, source_target_pairs={{1,0},{2,1},{3,2},{4,3},{5,4},{6,5},{7,6},{8,7},{9,8},{10,9},{11,1... | collective-permute-start | bytes 196616 | tf_op jit(solution)/shard_map/ppermute | solution.py:24
  96.1 0.7 copy-start.4
  96.1 0.7 copy-start.5
  99.4 1.1 copy-start.3
  101.9 32.8 %all-to-all-start = ((f32[2,2,32,1280]{3,1,0,2:T(2,128)}), f32[2,2,32,1280]{3,1,0,2:T(2,128)S(1)}, u32[]{:S(2)}, u32[]{:S(2)}) async-start(f32[2,2,32,1280]{3,1,0,2:T(2,128)} %copy.10), calls=%async_computation | async-start | bytes 1310720 | tf_op jit(solution)/shard_map/all_to_all | solution.py:65
where the time goes:
time: 276 us
  blocking collectives  125 us (45%)
  starting transfers between devices  89.9 us (33%)
  waiting for transfers between devices  25 us (9%)
  other arithmetic  17.6 us (6%)
  local copies, waits for them, and re-layouts  15.7 us (6%)
    psum x1, blocking collectives, on_device(): packed = lax.psum(packed, ('band', 'grid')) * inverse_cells  125 us
    ppermute x5, starting transfers between devices, padded_2(): lax.ppermute(head, axis, [((i + 1) % count, i) for i in range(count)])  67.2 us
    all_to_all x1, waiting for transfers between devices, on_device(): moved = lax.all_to_all(both, 'band', 2, 1, tiled=True)  22.4 us
    ppermute x5, starting transfers between devices, padded_2(): lax.ppermute(tail, axis, [(i, (i + 1) % count) for i in range(count)])  12.3 us
    all_to_all x1, starting transfers between devices, on_device(): moved = lax.all_to_all(both, 'band', 2, 1, tiled=True)  10.4 us
    another operation x3, other arithmetic, on_device(): factor = jnp.linalg.cholesky(margin)  6.52 us
    another operation x2, other arithmetic, on_device(): lax.linalg.triangular_solve(factor, coefficients.T, left_side=True, lower...  5.55 us
  transfers between devices with their start and end apart: 11, of which 4 were waited for; matrix products, arithmetic and copies ran while one was open for 1% of the time, Pallas kernels for 0%

commit v1 on v0

--- a/solution.py
+++ b/solution.py
@@ -10,6 +10,11 @@
 FOUR_THIRDS = 4.0 / 3.0
 TWELFTH = 1.0 / 12.0
 filter_degree = 4
+
+
+def axis_by_axis(array, first, second):
+    partial = lax.psum(array, first)
+    return lax.psum(partial, second)
 
 
 def padded_2(cells, sides, width):
@@ -79,7 +84,7 @@
     )
     norm_part = jnp.sum(image_here * image_here, axis=1)
     packed = jnp.concatenate([margin_part.reshape(-1), image_part.reshape(-1), norm_part])
-    packed = lax.psum(packed, ("band", "grid")) * inverse_cells
+    packed = axis_by_axis(packed, "band", "grid") * inverse_cells
     square = total_bands * total_bands
     margin = packed[:square].reshape(total_bands, total_bands)
     subspace = packed[square : 2 * square].reshape(total_bands, total_bands)

time: 276 us -> 513 us (1.86); the launches traced: 276 us -> 503 us
  blocking collectives: 125 us -> 352 us
    psum x1 -> x2, blocking collectives: 125 us -> 352 us  [the longest x1 200 us: axis_by_axis(): partial = lax.psum(array, first)]
where the time goes in v1:
time: 513 us; the launch traced here: 503 us
  blocking collectives  352 us (69%)
  starting transfers between devices  89.9 us (18%)
  waiting for transfers between devices  25 us (5%)
  other arithmetic  17.6 us (3%)
  local copies, waits for them, and re-layouts  15.7 us (3%)
    psum x1, blocking collectives, axis_by_axis(): partial = lax.psum(array, first)  200 us
    psum x1, blocking collectives, axis_by_axis(): return lax.psum(partial, second)  152 us
    ppermute x5, starting transfers between devices, padded_2(): lax.ppermute(head, axis, [((i + 1) % count, i) for i in range(count)])  67.2 us
    all_to_all x1, waiting for transfers between devices, on_device(): moved = lax.all_to_all(both, 'band', 2, 1, tiled=True)  22.4 us
    ppermute x5, starting transfers between devices, padded_2(): lax.ppermute(tail, axis, [(i, (i + 1) % count) for i in range(count)])  12.3 us
    all_to_all x1, starting transfers between devices, on_device(): moved = lax.all_to_all(both, 'band', 2, 1, tiled=True)  10.4 us
  transfers between devices with their start and end apart: 11, of which 4 were waited for; matrix products, arithmetic and copies ran while one was open for 1% of the time, Pallas kernels for 0%

profile of v1, /device:TPU:1, one launch (start us, length us, event | category | flops | bytes accessed | tf_op | source)
XLA Modules:
  0.0 503.0 jit_solution(14452085747746712297)
XLA Ops:
  0.6 0.9 fusion.146
  1.5 4.6 collective-permute-start
  6.1 6.2 %collective-permute-start.1 = (f32[2,2,32,128]{3,2,1,0:T(8,128)S(1)}, f32[2,2,32,128]{3,2,1,0:T(8,128)S(1)}, u32[]{:S(2)}, u32[]{:S(2)}) collective-permute-start(f32[2,2,32,128]{3,2,1,0:T(8,128)S(1)} %get-tuple-element.92), channel_id=1, source_target_pairs={{1,0},{2,1},{3,2},{4,3},{5,4},{6,5},{7,6},{8,7},{9,8},{10,9},{11,1... | collective-permute-start | bytes 196616 | tf_op jit(solution)/shard_map/ppermute | solution.py:29
  12.4 1.2 fusion.150
  13.8 0.2 fusion.145
  14.3 0.7 copy-done.2
  15.2 0.7 broadcast_multiply_fusion
  16.0 0.2 fusion.134
  16.7 1.9 collective-permute-start.2
  18.6 14.5 %collective-permute-start.3 = (f32[2,2,32,128]{3,2,1,0:T(8,128)S(1)}, f32[2,2,32,128]{3,2,1,0:T(8,128)S(1)}, u32[]{:S(2)}, u32[]{:S(2)}) collective-permute-start(f32[2,2,32,128]{3,2,1,0:T(8,128)S(1)} %get-tuple-element.80), channel_id=1, source_target_pairs={{1,0},{2,1},{3,2},{4,3},{5,4},{6,5},{7,6},{8,7},{9,8},{10,9},{11,1... | collective-permute-start | bytes 196616 | tf_op jit(solution)/shard_map/ppermute | solution.py:29
  33.1 0.8 collective-permute-done.3
  34.0 0.7 fusion.55
  35.5 1.9 collective-permute-start.4
  37.4 15.5 %collective-permute-start.5 = (f32[2,2,32,128]{3,2,1,0:T(8,128)S(1)}, f32[2,2,32,128]{3,2,1,0:T(8,128)S(1)}, u32[]{:S(2)}, u32[]{:S(2)}) collective-permute-start(f32[2,2,32,128]{3,2,1,0:T(8,128)S(1)} %get-tuple-element.62), channel_id=1, source_target_pairs={{1,0},{2,1},{3,2},{4,3},{5,4},{6,5},{7,6},{8,7},{9,8},{10,9},{11,1... | collective-permute-start | bytes 196616 | tf_op jit(solution)/shard_map/ppermute | solution.py:29
  52.9 0.8 collective-permute-done.5
  53.8 0.6 fusion.40
  55.2 1.9 collective-permute-start.6
  57.2 15.5 %collective-permute-start.7 = (f32[2,2,32,128]{3,2,1,0:T(8,128)S(1)}, f32[2,2,32,128]{3,2,1,0:T(8,128)S(1)}, u32[]{:S(2)}, u32[]{:S(2)}) collective-permute-start(f32[2,2,32,128]{3,2,1,0:T(8,128)S(1)} %get-tuple-element.44), channel_id=1, source_target_pairs={{1,0},{2,1},{3,2},{4,3},{5,4},{6,5},{7,6},{8,7},{9,8},{10,9},{11,1... | collective-permute-start | bytes 196616 | tf_op jit(solution)/shard_map/ppermute | solution.py:29
  72.7 0.8 collective-permute-done.7
  73.6 0.6 fusion.25
  74.8 0.9 fusion.111
  75.7 0.9 fusion.112
  76.7 0.7 fusion.114
  77.3 1.9 collective-permute-start.8
  79.3 15.5 %collective-permute-start.9 = (f32[2,2,32,128]{3,2,1,0:T(8,128)}, f32[2,2,32,128]{3,2,1,0:T(8,128)}, u32[]{:S(2)}, u32[]{:S(2)}) collective-permute-start(f32[2,2,32,128]{3,2,1,0:T(8,128)} %get-tuple-element.26), channel_id=1, source_target_pairs={{1,0},{2,1},{3,2},{4,3},{5,4},{6,5},{7,6},{8,7},{9,8},{10,9},{11,1... | collective-permute-start | bytes 196616 | tf_op jit(solution)/shard_map/ppermute | solution.py:29
  94.8 0.6 fusion.113
  95.4 0.8 stack.7
  96.2 0.7 copy-done.4
  96.9 2.5 fusion.10
  99.5 1.1 stack.8
  100.6 1.4 copy.10
  102.0 10.4 %all-to-all-start = ((f32[2,2,32,1280]{3,1,0,2:T(2,128)}), f32[2,2,32,1280]{3,1,0,2:T(2,128)S(1)}, u32[]{:S(2)}, u32[]{:S(2)}) async-start(f32[2,2,32,1280]{3,1,0,2:T(2,128)} %copy.10), calls=%async_computation | async-start | bytes 1310720 | tf_op jit(solution)/shard_map/all_to_all | solution.py:70
  112.3 22.4 %all-to-all-done = f32[2,2,32,1280]{3,1,0,2:T(2,128)S(1)} async-done(((f32[2,2,32,1280]{3,1,0,2:T(2,128)}), f32[2,2,32,1280]{3,1,0,2:T(2,128)S(1)}, u32[]{:S(2)}, u32[]{:S(2)}) %all-to-all-start) | async-done | bytes 655392 | tf_op jit(solution)/shard_map/all_to_all | solution.py:70
  134.8 0.3 fusion.105
  135.0 0.2 reshape_squeeze.6
  135.3 0.2 reshape_squeeze.7
  135.5 0.4 fusion.152
  135.9 0.4 fusion.153
  136.6 200.3 %psum.14 = f32[8256]{0:T(1024)S(1)} all-reduce(f32[8256]{0:T(1024)S(1)} %pad_maximum_fusion.9), channel_id=1, replica_groups=mesh['band'=32,'grid'=16] {'band'}, use_global_device_ids=true, to_apply=%region_1.2 | all-reduce | flops 8256 | bytes 66048 | tf_op jit(solution)/shard_map/psum | solution.py:16
  336.9 152.1 %psum.15 = f32[8256]{0:T(1024)S(1)} all-reduce(f32[8256]{0:T(1024)S(1)} %psum.14), channel_id=1, replica_groups=mesh['band'=32,'grid'=16] {'grid'}, use_global_device_ids=true, to_apply=%region_2.3 | all-reduce | flops 8256 | bytes 66048 | tf_op jit(solution)/shard_map/psum | solution.py:17
  489.2 5.8 %cholesky.18 = f32[64,64]{1,0:T(8,128)S(1)} custom-call(f32[64,64]{1,0:T(8,128)S(1)} %fusion.103), custom_call_target="Cholesky" | custom-call | tf_op jit(solution)/shard_map/jit(cholesky)/cholesky | solution.py:92
  495.1 0.6 compare_reduce_fusion
  495.7 0.7 fusion.96
  496.4 4.9 custom-call.8
  501.4 0.3 multiply_reduce_fusion.1
  501.6 0.2 fusion.97
  501.9 0.6 dynamic_slice.7
  502.5 0.6 constant_dynamic-slice_fusion
  (71 shorter events, 4.1 us)
Async XLA Ops:
  1.5 13.5 %collective-permute-start = (f32[2,2,32,128]{3,2,1,0:T(8,128)S(1)}, f32[2,2,32,128]{3,2,1,0:T(8,128)S(1)}, u32[]{:S(2)}, u32[]{:S(2)}) collective-permute-start(f32[2,2,32,128]{3,2,1,0:T(8,128)S(1)} %get-tuple-element.91), channel_id=1, source_target_pairs={{0,1},{1,2},{2,3},{3,4},{4,5},{5,6},{6,7},{7,8},{8,9},{9,10},{10,1... | collective-permute-start | bytes 196616 | tf_op jit(solution)/shard_map/ppermute | solution.py:27
  6.1 7.5 %copy-start.1 = (f32[2,10,32,128]{3,2,1,0:T(8,128)S(1)}, f32[2,10,32,128]{3,2,1,0:T(8,128)}, u32[]{:S(2)}) copy-start(f32[2,10,32,128]{3,2,1,0:T(8,128)} %param.4) | copy-start | bytes 983044
  6.1 9.0 %collective-permute-start.1 = (f32[2,2,32,128]{3,2,1,0:T(8,128)S(1)}, f32[2,2,32,128]{3,2,1,0:T(8,128)S(1)}, u32[]{:S(2)}, u32[]{:S(2)}) collective-permute-start(f32[2,2,32,128]{3,2,1,0:T(8,128)S(1)} %get-tuple-element.92), channel_id=1, source_target_pairs={{1,0},{2,1},{3,2},{4,3},{5,4},{6,5},{7,6},{8,7},{9,8},{10,9},{11,1... | collective-permute-start | bytes 196616 | tf_op jit(solution)/shard_map/ppermute | solution.py:29
  14.1 0.9 copy-start.2
  16.7 16.4 %collective-permute-start.2 = (f32[2,2,32,128]{3,2,1,0:T(8,128)S(1)}, f32[2,2,32,128]{3,2,1,0:T(8,128)S(1)}, u32[]{:S(2)}, u32[]{:S(2)}) collective-permute-start(f32[2,2,32,128]{3,2,1,0:T(8,128)S(1)} %get-tuple-element.79), channel_id=1, source_target_pairs={{0,1},{1,2},{2,3},{3,4},{4,5},{5,6},{6,7},{7,8},{8,9},{9,10},{10,1... | collective-permute-start | bytes 196616 | tf_op jit(solution)/shard_map/ppermute | solution.py:27
  18.6 15.4 %collective-permute-start.3 = (f32[2,2,32,128]{3,2,1,0:T(8,128)S(1)}, f32[2,2,32,128]{3,2,1,0:T(8,128)S(1)}, u32[]{:S(2)}, u32[]{:S(2)}) collective-permute-start(f32[2,2,32,128]{3,2,1,0:T(8,128)S(1)} %get-tuple-element.80), channel_id=1, source_target_pairs={{1,0},{2,1},{3,2},{4,3},{5,4},{6,5},{7,6},{8,7},{9,8},{10,9},{11,1... | collective-permute-start | bytes 196616 | tf_op jit(solution)/shard_map/ppermute | solution.py:29
  35.5 17.4 %collective-permute-start.4 = (f32[2,2,32,128]{3,2,1,0:T(8,128)S(1)}, f32[2,2,32,128]{3,2,1,0:T(8,128)S(1)}, u32[]{:S(2)}, u32[]{:S(2)}) collective-permute-start(f32[2,2,32,128]{3,2,1,0:T(8,128)S(1)} %get-tuple-element.61), channel_id=1, source_target_pairs={{0,1},{1,2},{2,3},{3,4},{4,5},{5,6},{6,7},{7,8},{8,9},{9,10},{10,1... | collective-permute-start | bytes 196616 | tf_op jit(solution)/shard_map/ppermute | solution.py:27
  37.4 16.4 %collective-permute-start.5 = (f32[2,2,32,128]{3,2,1,0:T(8,128)S(1)}, f32[2,2,32,128]{3,2,1,0:T(8,128)S(1)}, u32[]{:S(2)}, u32[]{:S(2)}) collective-permute-start(f32[2,2,32,128]{3,2,1,0:T(8,128)S(1)} %get-tuple-element.62), channel_id=1, source_target_pairs={{1,0},{2,1},{3,2},{4,3},{5,4},{6,5},{7,6},{8,7},{9,8},{10,9},{11,1... | collective-permute-start | bytes 196616 | tf_op jit(solution)/shard_map/ppermute | solution.py:29
  55.2 17.5 %collective-permute-start.6 = (f32[2,2,32,128]{3,2,1,0:T(8,128)S(1)}, f32[2,2,32,128]{3,2,1,0:T(8,128)S(1)}, u32[]{:S(2)}, u32[]{:S(2)}) collective-permute-start(f32[2,2,32,128]{3,2,1,0:T(8,128)S(1)} %get-tuple-element.43), channel_id=1, source_target_pairs={{0,1},{1,2},{2,3},{3,4},{4,5},{5,6},{6,7},{7,8},{8,9},{9,10},{10,1... | collective-permute-start | bytes 196616 | tf_op jit(solution)/shard_map/ppermute | solution.py:27
  57.2 16.4 %collective-permute-start.7 = (f32[2,2,32,128]{3,2,1,0:T(8,128)S(1)}, f32[2,2,32,128]{3,2,1,0:T(8,128)S(1)}, u32[]{:S(2)}, u32[]{:S(2)}) collective-permute-start(f32[2,2,32,128]{3,2,1,0:T(8,128)S(1)} %get-tuple-element.44), channel_id=1, source_target_pairs={{1,0},{2,1},{3,2},{4,3},{5,4},{6,5},{7,6},{8,7},{9,8},{10,9},{11,1... | collective-permute-start | bytes 196616 | tf_op jit(solution)/shard_map/ppermute | solution.py:29
  74.2 22.0 %copy-start = (f32[2,10,32,128]{3,2,1,0:T(8,128)}, f32[2,10,32,128]{3,2,1,0:T(8,128)S(1)}, u32[]{:S(2)}) copy-start(f32[2,10,32,128]{3,2,1,0:T(8,128)S(1)} %fusion.25) | copy-start | bytes 983044
  77.3 18.9 %collective-permute-start.8 = (f32[2,2,32,128]{3,2,1,0:T(8,128)}, f32[2,2,32,128]{3,2,1,0:T(8,128)S(1)}, u32[]{:S(2)}, u32[]{:S(2)}) collective-permute-start(f32[2,2,32,128]{3,2,1,0:T(8,128)} %get-tuple-element.25), channel_id=1, source_target_pairs={{0,1},{1,2},{2,3},{3,4},{4,5},{5,6},{6,7},{7,8},{8,9},{9,10},{10,1... | collective-permute-start | bytes 196616 | tf_op jit(solution)/shard_map/ppermute | solution.py:27
  79.3 16.9 %collective-permute-start.9 = (f32[2,2,32,128]{3,2,1,0:T(8,128)}, f32[2,2,32,128]{3,2,1,0:T(8,128)}, u32[]{:S(2)}, u32[]{:S(2)}) collective-permute-start(f32[2,2,32,128]{3,2,1,0:T(8,128)} %get-tuple-element.26), channel_id=1, source_target_pairs={{1,0},{2,1},{3,2},{4,3},{5,4},{6,5},{7,6},{8,7},{9,8},{10,9},{11,1... | collective-permute-start | bytes 196616 | tf_op jit(solution)/shard_map/ppermute | solution.py:29
  96.2 0.7 copy-start.4
  96.2 0.7 copy-start.5
  99.4 1.1 copy-start.3
  102.0 32.8 %all-to-all-start = ((f32[2,2,32,1280]{3,1,0,2:T(2,128)}), f32[2,2,32,1280]{3,1,0,2:T(2,128)S(1)}, u32[]{:S(2)}, u32[]{:S(2)}) async-start(f32[2,2,32,1280]{3,1,0,2:T(2,128)} %copy.10), calls=%async_computation | async-start | bytes 1310720 | tf_op jit(solution)/shard_map/all_to_all | solution.py:70
